TPU v7x, 32 devices: a whole 2x2x4 slice. The times are simulated.
32 devices in a mesh: rows: 16 (over z, y, x), grp: 2 (over core).
Axes of the slice: x: 2, y: 2, z: 4, core: 2. Of those that a mesh axis runs over, the one named last changes fastest.
Arguments:
- slab_x: bfloat16 [131072, 512], P(('rows', 'grp'))
- slab_y: bfloat16 [131072, 256], P(('rows', 'grp')), may hold values from -6 to 6
- row_mask: int32 [131072], P(('rows', 'grp')), may hold values 0 or 1
- live_tiles: int32 [32], P(('rows', 'grp')), may hold values from 1 to 32, as said below
- old_r: float32 [512, 512], P('rows'), as said below
- old_z: float32 [512, 256], P('rows'), may hold values from -6 to 6
Outputs:
- new_r: float32 [512, 512], replicated
- new_z: float32 [512, 256], replicated
Inputs may be any that keep to these rules, and one draw needn't show every extreme that they name: `live_tiles`: live tiles of each device; at least one device has all 32. old_r is upper triangular with diagonal entries from 0.5 to 2.
All inputs are finite; a program needn't handle non-finite values. No bound on the sum of `row_mask` on one device may be relied on, other than what follows from the above.
Results may differ from a plain program's by a relative error of at most 0.0003.
Values sent between devices are 32-bit elements; how exact they have to be, the bound alone decides.
No kernel may reach another device: no remote copies, remote signals or barrier semaphores. Data moves between devices by JAX's collectives and lax.ppermute only.
A program may use at most 64 MiB of HBM per device.

v0:
```python
import jax
import jax.numpy as jnp
from jax import lax
from jax.sharding import PartitionSpec as P

TILE = 128
AXES = ("rows", "grp")


def contract(left, right, precision=None):
    return lax.dot_general(
        left,
        right,
        (((0,), (0,)), ((), ())),
        precision=precision,
        preferred_element_type=jnp.float32,
    )


def butterfly_sum(local, n_dev):
    idx = lax.axis_index(AXES)
    steps = n_dev.bit_length() - 1
    cur = local
    for k in range(steps):
        pairs = [(i, i ^ (1 << k)) for i in range(n_dev)]
        half = cur.shape[0] // 2
        low = ((idx >> k) & 1) == 0
        lo, hi = cur[:half], cur[half:]
        keep = jnp.where(low, lo, hi)
        send = jnp.where(low, hi, lo)
        cur = keep + lax.ppermute(send, AXES, pairs)
    for k in reversed(range(steps)):
        pairs = [(i, i ^ (1 << k)) for i in range(n_dev)]
        low = ((idx >> k) & 1) == 0
        got = lax.ppermute(cur, AXES, pairs)
        cur = jnp.where(low, jnp.concatenate([cur, got]), jnp.concatenate([got, cur]))
    return cur


def summed(local, n_dev):
    rows = local.shape[0]
    if n_dev & (n_dev - 1) == 0 and rows % n_dev == 0:
        return butterfly_sum(local, n_dev)
    return lax.psum(local, AXES)


def body(slab_x, slab_y, row_mask, live_tiles, old_r, old_z):
    rows_here, width = slab_x.shape
    n_grp = lax.axis_size("grp")
    n_dev = lax.axis_size("rows") * n_grp
    tile_ids = lax.broadcasted_iota(jnp.int32, (rows_here,), 0) // TILE
    live = (row_mask == 1) & (tile_ids < live_tiles[0])
    masked = jnp.where(live[:, None], slab_x, jnp.zeros_like(slab_x))
    gram = contract(masked, slab_x)
    cross = contract(masked, slab_y)
    share = old_r.shape[0] // n_grp
    start = lax.axis_index("grp") * share
    r_part = lax.dynamic_slice_in_dim(old_r, start, share, 0)
    z_part = lax.dynamic_slice_in_dim(old_z, start, share, 0)
    gram = gram + contract(r_part, r_part, lax.Precision.HIGHEST)
    cross = cross + contract(r_part, z_part, lax.Precision.HIGHEST)
    both = summed(jnp.concatenate([gram, cross], axis=1), n_dev)
    total = both[:, :width]
    rhs = both[:, width:]
    return factor_and_solve(total, rhs)


def factor_and_solve(total, rhs, block=128):
    n = total.shape[0]
    trail = jnp.concatenate([total, rhs.T], axis=0)
    columns = []
    for s in range(0, n, block):
        diag = lax.linalg.cholesky(trail[:block, :block], symmetrize_input=False)
        diag = jnp.tril(diag)
        panel = lax.linalg.triangular_solve(
            diag, trail[block:, :block], left_side=False, lower=True, transpose_a=True
        )
        columns.append(jnp.concatenate([diag, panel], axis=0))
        if s + block < n:
            upper = panel[: n - s - block]
            trail = trail[block:, block:] - lax.dot_general(
                panel,
                upper,
                (((1,), (1,)), ((), ())),
                precision=lax.Precision.HIGHEST,
                preferred_element_type=jnp.float32,
            )
    lower = jnp.concatenate(
        [jnp.pad(col[: n - s], ((s, 0), (0, 0))) for s, col in zip(range(0, n, block), columns)],
        axis=1,
    )
    new_z_t = jnp.concatenate([col[n - s :] for s, col in zip(range(0, n, block), columns)], axis=1)
    return (lower.T, new_z_t.T)


def solution(mesh):
    placed = (
        P(AXES, None),
        P(AXES, None),
        P(AXES),
        P(AXES),
        P("rows", None),
        P("rows", None),
    )
    return jax.shard_map(body, mesh=mesh, in_specs=placed, out_specs=(P(), P()), check_vma=False)
```

profile of v0, /device:TPU:0, one launch (start us, length us, event | category | flops | bytes accessed | tf_op | source)
XLA Modules:
  0.0 253.5 jit_solution(18283744839667551146)
XLA Ops:
  2.2 7.4 %fusion.2 = f32[512,512]{0,1:T(8,128)} fusion(bf16[4096,512]{1,0:T(8,128)(2,1)} %param.7, pred[4096]{0:T(1024)(128)(4,1)S(1)} %fusion.40), kind=kOutput, calls=%fused_computation.2 | convolution fusion | flops 2149580800 | bytes 5246976 | tf_op jit(solution)/shard_map/dot_general | solution.py:11
  9.6 2.6 %fusion = f32[512,256]{0,1:T(8,128)} fusion(bf16[4096,256]{1,0:T(8,128)(2,1)S(1)} %copy-done, bf16[4096,512]{1,0:T(8,128)(2,1)S(1)} %copy-done.12, pred[4096]{0:T(1024)(128)(4,1)S(1)} %fusion.40), kind=kOutput, calls=%fused_computation | convolution fusion | flops 1075838976 | bytes 6819840 | tf_op jit(solution)/shard_map/dot_general | solution.py:11
  12.2 2.3 convolution_add_fusion
  17.4 2.3 collective-permute-done
  22.0 2.9 %collective-permute-start.1 = (f32[128,768]{0,1:T(8,128)S(1)}, f32[128,768]{0,1:T(8,128)S(1)}, u32[]{:S(2)}, u32[]{:S(2)}) collective-permute-start(f32[128,768]{0,1:T(8,128)S(1)} %slice_select_fusion.3), channel_id=1, source_target_pairs={{0,2},{1,3},{2,0},{3,1},{4,6},{5,7},{6,4},{7,5},{8,10},{9,11},{10,... | collective-permute-start | bytes 1179656 | tf_op jit(solution)/shard_map/ppermute | solution.py:31
  24.9 9.4 %collective-permute-done.1 = f32[128,768]{0,1:T(8,128)S(1)} collective-permute-done((f32[128,768]{0,1:T(8,128)S(1)}, f32[128,768]{0,1:T(8,128)S(1)}, u32[]{:S(2)}, u32[]{:S(2)}) %collective-permute-start.1) | collective-permute-done | bytes 393248 | tf_op jit(solution)/shard_map/ppermute | solution.py:31
  37.5 8.9 %collective-permute-done.2 = f32[64,768]{0,1:T(8,128)S(1)} collective-permute-done((f32[64,768]{0,1:T(8,128)S(1)}, f32[64,768]{0,1:T(8,128)S(1)}, u32[]{:S(2)}, u32[]{:S(2)}) %collective-permute-start.2) | collective-permute-done | bytes 196640 | tf_op jit(solution)/shard_map/ppermute | solution.py:31
  48.3 8.2 %collective-permute-done.3 = f32[32,768]{0,1:T(8,128)S(1)} collective-permute-done((f32[32,768]{0,1:T(8,128)S(1)}, f32[32,768]{0,1:T(8,128)S(1)}, u32[]{:S(2)}, u32[]{:S(2)}) %collective-permute-start.3) | collective-permute-done | bytes 98336 | tf_op jit(solution)/shard_map/ppermute | solution.py:31
  56.9 2.2 collective-permute-start.4
  59.1 16.0 %collective-permute-done.4 = f32[16,768]{0,1:T(8,128)S(1)} collective-permute-done((f32[16,768]{0,1:T(8,128)S(1)}, f32[16,768]{0,1:T(8,128)S(1)}, u32[]{:S(2)}, u32[]{:S(2)}) %collective-permute-start.4) | collective-permute-done | bytes 49184 | tf_op jit(solution)/shard_map/ppermute | solution.py:31
  75.3 20.0 %collective-permute-done.5 = f32[16,768]{0,1:T(8,128)S(1)} collective-permute-done((f32[16,768]{0,1:T(8,128)S(1)}, f32[16,768]{0,1:T(8,128)S(1)}, u32[]{:S(2)}, u32[]{:S(2)}) %collective-permute-start.5) | collective-permute-done | bytes 49184 | tf_op jit(solution)/shard_map/ppermute | solution.py:35
  95.7 10.6 %collective-permute-done.6 = f32[32,768]{0,1:T(8,128)S(1)} collective-permute-done((f32[32,768]{0,1:T(8,128)S(1)}, f32[32,768]{0,1:T(8,128)S(1)}, u32[]{:S(2)}, u32[]{:S(2)}) %collective-permute-start.6) | collective-permute-done | bytes 98336 | tf_op jit(solution)/shard_map/ppermute | solution.py:35
  106.6 9.6 %collective-permute-done.7 = f32[64,768]{0,1:T(8,128)S(1)} collective-permute-done((f32[64,768]{0,1:T(8,128)S(1)}, f32[64,768]{0,1:T(8,128)S(1)}, u32[]{:S(2)}, u32[]{:S(2)}) %collective-permute-start.7) | collective-permute-done | bytes 196640 | tf_op jit(solution)/shard_map/ppermute | solution.py:35
  116.6 8.7 %collective-permute-done.8 = f32[128,768]{0,1:T(8,128)S(1)} collective-permute-done((f32[128,768]{0,1:T(8,128)S(1)}, f32[128,768]{0,1:T(8,128)S(1)}, u32[]{:S(2)}, u32[]{:S(2)}) %collective-permute-start.8) | collective-permute-done | bytes 393248 | tf_op jit(solution)/shard_map/ppermute | solution.py:35
  125.5 2.3 collective-permute-done.9
  129.9 11.9 %custom-call.22 = f32[128,128]{1,0:T(8,128)S(1)} custom-call(f32[128,128]{1,0:T(8,128)S(1)} %copy.24), custom_call_target="Cholesky" | custom-call | tf_op jit(solution)/shard_map/cholesky/custom-call.1 | solution.py:73
  144.0 9.8 %custom-call.15 = f32[1,128,128]{1,2,0:T(8,128)S(1)} custom-call(f32[1,128,128]{2,1,0:T(8,128)S(1)} %get-tuple-element.15), custom_call_target="InvertDiagBlocksLowerTriangular" | custom-call | tf_op jit(solution)/shard_map/triangular_solve | solution.py:75
  158.7 11.7 %custom-call.23 = f32[128,128]{1,0:T(8,128)S(1)} custom-call(f32[128,128]{1,0:T(8,128)S(1)} %slice.153), custom_call_target="Cholesky" | custom-call | tf_op jit(solution)/shard_map/cholesky/custom-call.1 | solution.py:73
  172.4 9.8 %custom-call.16 = f32[1,128,128]{1,2,0:T(8,128)S(1)} custom-call(f32[1,128,128]{2,1,0:T(8,128)S(1)} %get-tuple-element.13), custom_call_target="InvertDiagBlocksLowerTriangular" | custom-call | tf_op jit(solution)/shard_map/triangular_solve | solution.py:75
  185.9 20.7 %custom-call.24 = f32[128,128]{1,0:T(8,128)S(1)} custom-call(f32[128,128]{1,0:T(8,128)S(1)} %slice.156), custom_call_target="Cholesky" | custom-call | tf_op jit(solution)/shard_map/cholesky/custom-call.1 | solution.py:73
  208.6 9.8 %custom-call.17 = f32[1,128,128]{1,2,0:T(8,128)S(1)} custom-call(f32[1,128,128]{2,1,0:T(8,128)S(1)} %get-tuple-element.11), custom_call_target="InvertDiagBlocksLowerTriangular" | custom-call | tf_op jit(solution)/shard_map/triangular_solve | solution.py:75
  222.3 11.7 %custom-call.25 = f32[128,128]{1,0:T(8,128)S(1)} custom-call(f32[128,128]{1,0:T(8,128)S(1)} %slice.159), custom_call_target="Cholesky" | custom-call | tf_op jit(solution)/shard_map/cholesky/custom-call.1 | solution.py:73
  235.9 9.8 %custom-call.18 = f32[1,128,128]{1,2,0:T(8,128)S(1)} custom-call(f32[1,128,128]{2,1,0:T(8,128)S(1)} %get-tuple-element.9), custom_call_target="InvertDiagBlocksLowerTriangular" | custom-call | tf_op jit(solution)/shard_map/triangular_solve | solution.py:75
  250.8 2.5 copy.27
  (86 shorter events, 40.3 us)
Async XLA Ops:
  0.6 8.9 %copy-start = (bf16[4096,256]{1,0:T(8,128)(2,1)S(1)}, bf16[4096,256]{1,0:T(8,128)(2,1)}, u32[]{:S(2)}) copy-start(bf16[4096,256]{1,0:T(8,128)(2,1)} %param.8) | copy-start | bytes 6291460
  2.2 7.4 %copy-start.12 = (bf16[4096,512]{1,0:T(8,128)(2,1)S(1)}, bf16[4096,512]{1,0:T(8,128)(2,1)}, u32[]{:S(2)}) copy-start(bf16[4096,512]{1,0:T(8,128)(2,1)} %param.7) | copy-start | bytes 12582916
  9.6 2.6 %copy-start.10 = (f32[32,512]{1,0:T(8,128)S(1)}, f32[32,512]{1,0:T(8,128)}, u32[]{:S(2)}) copy-start(f32[32,512]{1,0:T(8,128)} %param.11) | copy-start | bytes 196612
  12.2 2.3 copy-start.11
  12.2 2.3 copy-start.8
  15.1 0.8 copy-start.4
  16.9 2.7 %collective-permute-start = (f32[256,768]{0,1:T(8,128)}, f32[256,768]{0,1:T(8,128)}, u32[]{:S(2)}, u32[]{:S(2)}) collective-permute-start(f32[256,768]{0,1:T(8,128)} %broadcast_select_fusion), channel_id=1, source_target_pairs={{0,1},{1,0},{2,3},{3,2},{4,5},{5,4},{6,7},{7,6},{8,9},{9,8},{10,11... | collective-permute-start | bytes 2359304 | tf_op jit(solution)/shard_map/ppermute | solution.py:31
  21.0 0.9 copy-start.1
  22.0 12.3 %collective-permute-start.1 = (f32[128,768]{0,1:T(8,128)S(1)}, f32[128,768]{0,1:T(8,128)S(1)}, u32[]{:S(2)}, u32[]{:S(2)}) collective-permute-start(f32[128,768]{0,1:T(8,128)S(1)} %slice_select_fusion.3), channel_id=1, source_target_pairs={{0,2},{1,3},{2,0},{3,1},{4,6},{5,7},{6,4},{7,5},{8,10},{9,11},{10,... | collective-permute-start | bytes 1179656 | tf_op jit(solution)/shard_map/ppermute | solution.py:31
  35.6 10.7 %collective-permute-start.2 = (f32[64,768]{0,1:T(8,128)S(1)}, f32[64,768]{0,1:T(8,128)S(1)}, u32[]{:S(2)}, u32[]{:S(2)}) collective-permute-start(f32[64,768]{0,1:T(8,128)S(1)} %slice_select_fusion.2), channel_id=1, source_target_pairs={{0,4},{1,5},{2,6},{3,7},{4,0},{5,1},{6,2},{7,3},{8,12},{9,13},{10,... | collective-permute-start | bytes 589832 | tf_op jit(solution)/shard_map/ppermute | solution.py:31
  46.7 9.8 %collective-permute-start.3 = (f32[32,768]{0,1:T(8,128)S(1)}, f32[32,768]{0,1:T(8,128)S(1)}, u32[]{:S(2)}, u32[]{:S(2)}) collective-permute-start(f32[32,768]{0,1:T(8,128)S(1)} %slice_select_fusion.1), channel_id=1, source_target_pairs={{0,8},{1,9},{2,10},{3,11},{4,12},{5,13},{6,14},{7,15},{8,0},{9,1},... | collective-permute-start | bytes 294920 | tf_op jit(solution)/shard_map/ppermute | solution.py:31
  56.9 18.2 %collective-permute-start.4 = (f32[16,768]{0,1:T(8,128)S(1)}, f32[16,768]{0,1:T(8,128)S(1)}, u32[]{:S(2)}, u32[]{:S(2)}) collective-permute-start(f32[16,768]{0,1:T(8,128)S(1)} %slice_select_fusion), channel_id=1, source_target_pairs={{0,16},{1,17},{2,18},{3,19},{4,20},{5,21},{6,22},{7,23},{8,24},{9,... | collective-permute-start | bytes 147464 | tf_op jit(solution)/shard_map/ppermute | solution.py:31
  75.2 20.1 %collective-permute-start.5 = (f32[16,768]{0,1:T(8,128)S(1)}, f32[16,768]{0,1:T(8,128)S(1)}, u32[]{:S(2)}, u32[]{:S(2)}) collective-permute-start(f32[16,768]{0,1:T(8,128)S(1)} %select_add_fusion.1), channel_id=1, source_target_pairs={{0,16},{1,17},{2,18},{3,19},{4,20},{5,21},{6,22},{7,23},{8,24},{9,... | collective-permute-start | bytes 147464 | tf_op jit(solution)/shard_map/ppermute | solution.py:35
  95.6 10.6 %collective-permute-start.6 = (f32[32,768]{0,1:T(8,128)S(1)}, f32[32,768]{0,1:T(8,128)S(1)}, u32[]{:S(2)}, u32[]{:S(2)}) collective-permute-start(f32[32,768]{0,1:T(8,128)S(1)} %maximum_select_fusion.2), channel_id=1, source_target_pairs={{0,8},{1,9},{2,10},{3,11},{4,12},{5,13},{6,14},{7,15},{8,0},{9,1},... | collective-permute-start | bytes 294920 | tf_op jit(solution)/shard_map/ppermute | solution.py:35
  106.5 9.7 %collective-permute-start.7 = (f32[64,768]{0,1:T(8,128)S(1)}, f32[64,768]{0,1:T(8,128)S(1)}, u32[]{:S(2)}, u32[]{:S(2)}) collective-permute-start(f32[64,768]{0,1:T(8,128)S(1)} %maximum_select_fusion.3), channel_id=1, source_target_pairs={{0,4},{1,5},{2,6},{3,7},{4,0},{5,1},{6,2},{7,3},{8,12},{9,13},{10,... | collective-permute-start | bytes 589832 | tf_op jit(solution)/shard_map/ppermute | solution.py:35
  116.5 8.8 %collective-permute-start.8 = (f32[128,768]{0,1:T(8,128)S(1)}, f32[128,768]{0,1:T(8,128)S(1)}, u32[]{:S(2)}, u32[]{:S(2)}) collective-permute-start(f32[128,768]{0,1:T(8,128)S(1)} %maximum_select_fusion.4), channel_id=1, source_target_pairs={{0,2},{1,3},{2,0},{3,1},{4,6},{5,7},{6,4},{7,5},{8,10},{9,11},{10,... | collective-permute-start | bytes 1179656 | tf_op jit(solution)/shard_map/ppermute | solution.py:35
  125.4 2.4 collective-permute-start.9
  155.4 1.4 copy-start.5
  156.8 26.7 %copy-start.2 = (f32[640,128]{1,0:T(8,128)}, f32[640,128]{1,0:T(8,128)S(1)}, u32[]{:S(2)}) copy-start(f32[640,128]{1,0:T(8,128)S(1)} %fusion.13) | copy-start | bytes 983044
  157.7 0.9 copy-start.6
  185.1 0.8 copy-start.7
  185.9 60.0 %slice-start = ((f32[640,128]{1,0:T(8,128)}), f32[256,128]{1,0:T(8,128)S(1)}, s32[]{:S(2)}) async-start(f32[640,128]{1,0:T(8,128)} %copy-done.2), calls=%async_computation | async-start | bytes 262144 | tf_op jit(solution)/shard_map/slice | solution.py:92
  221.6 27.3 %copy-start.3 = (f32[640,128]{1,0:T(8,128)S(1)}, f32[640,128]{1,0:T(8,128)}, u32[]{:S(2)}) copy-start(f32[640,128]{1,0:T(8,128)} %copy-done.2) | copy-start | bytes 983044
  247.0 1.9 copy-start.9
where the time goes:
time: 258 us; the launch traced here: 254 us
  other arithmetic  113 us (44%)
  waiting for transfers between devices  96 us (37%)
  matrix products  20.9 us (8%)
  local copies, waits for them, and re-layouts  11.8 us (5%)
  starting transfers between devices  9.38 us (4%)
    another operation x12, other arithmetic, factor_and_solve(): diag = lax.linalg.cholesky(trail[:block, :block], symmetrize_input=False)  58.9 us
    ppermute x5, waiting for transfers between devices, butterfly_sum(): got = lax.ppermute(cur, AXES, pairs)  51.2 us
    ppermute x5, waiting for transfers between devices, butterfly_sum(): cur = keep + lax.ppermute(send, AXES, pairs)  44.8 us
    another operation x8, other arithmetic, factor_and_solve(): lax.linalg.triangular_solve(diag, trail[block:, :block], left_side=False,...  44.3 us
    dot_general x4, matrix products, contract(): lax.dot_general(left, right, (((0,), (0,)), ((), ())), precision=precisio...  12.9 us
    ppermute x5, starting transfers between devices, butterfly_sum(): cur = keep + lax.ppermute(send, AXES, pairs)  9.03 us
    unnamed x28, local copies, waits for them, and re-layouts  6.96 us
  transfers between devices with their start and end apart: 10, of which 10 were waited for; matrix products, arithmetic and copies ran while one was open for 0% of the time, Pallas kernels for 0%

commit v1 on v0

--- a/solution.py
+++ b/solution.py
@@ -59,15 +59,13 @@
     z_part = lax.dynamic_slice_in_dim(old_z, start, share, 0)
     gram = gram + contract(r_part, r_part, lax.Precision.HIGHEST)
     cross = cross + contract(r_part, z_part, lax.Precision.HIGHEST)
-    both = summed(jnp.concatenate([gram, cross], axis=1), n_dev)
-    total = both[:, :width]
-    rhs = both[:, width:]
-    return factor_and_solve(total, rhs)
+    both = summed(jnp.concatenate([gram.T, cross.T], axis=0), n_dev)
+    return factor_and_solve(both[:width].T, both[width:])
 
 
-def factor_and_solve(total, rhs, block=128):
+def factor_and_solve(total, rhs_t, block=128):
     n = total.shape[0]
-    trail = jnp.concatenate([total, rhs.T], axis=0)
+    trail = jnp.concatenate([total, rhs_t], axis=0)
     columns = []
     for s in range(0, n, block):
         diag = lax.linalg.cholesky(trail[:block, :block], symmetrize_input=False)

time: 258 us -> 193 us (0.75); the launches traced: 254 us -> 192 us
  waiting for transfers between devices: 96 us -> 39.1 us
  other arithmetic: 113 us -> 100 us
  starting transfers between devices: 9.38 us -> 18.9 us
    ppermute x5, waiting for transfers between devices: 51.2 us -> 17.4 us  [butterfly_sum(): got = lax.ppermute(cur, AXES, pairs)]
    ppermute x5, waiting for transfers between devices: 44.8 us -> 21.7 us  [butterfly_sum(): cur = keep + lax.ppermute(send, AXES, pairs)]
    another operation x12, other arithmetic: 58.9 us -> 49.7 us  [factor_and_solve(): diag = lax.linalg.cholesky(trail[:block, :block], symmetrize_input=False)]
    ppermute x5, starting transfers between devices: 0.36 us -> 9.31 us  [butterfly_sum(): got = lax.ppermute(cur, AXES, pairs)]
where the time goes in v1:
time: 193 us; the launch traced here: 192 us
  other arithmetic  100 us (52%)
  waiting for transfers between devices  39.1 us (20%)
  matrix products  21 us (11%)
  starting transfers between devices  18.9 us (10%)
  local copies, waits for them, and re-layouts  11.3 us (6%)
    another operation x12, other arithmetic, factor_and_solve(): diag = lax.linalg.cholesky(trail[:block, :block], symmetrize_input=False)  49.7 us
    another operation x8, other arithmetic, factor_and_solve(): lax.linalg.triangular_solve(diag, trail[block:, :block], left_side=False,...  44.1 us
    ppermute x5, waiting for transfers between devices, butterfly_sum(): cur = keep + lax.ppermute(send, AXES, pairs)  21.7 us
    ppermute x5, waiting for transfers between devices, butterfly_sum(): got = lax.ppermute(cur, AXES, pairs)  17.4 us
    dot_general x4, matrix products, contract(): lax.dot_general(left, right, (((0,), (0,)), ((), ())), precision=precisio...  12.9 us
    ppermute x5, starting transfers between devices, butterfly_sum(): cur = keep + lax.ppermute(send, AXES, pairs)  9.57 us
    ppermute x5, starting transfers between devices, butterfly_sum(): got = lax.ppermute(cur, AXES, pairs)  9.31 us
    unnamed x28, local copies, waits for them, and re-layouts  6.22 us
  transfers between devices with their start and end apart: 10, of which 10 were waited for; matrix products, arithmetic and copies ran while one was open for 0% of the time, Pallas kernels for 0%

profile of v1, /device:TPU:0, one launch (start us, length us, event | category | flops | bytes accessed | tf_op | source)
XLA Modules:
  0.0 192.1 jit_solution(10596340582774451472)
XLA Ops:
  2.2 7.4 %fusion.8 = f32[512,512]{1,0:T(8,128)} fusion(bf16[4096,512]{1,0:T(8,128)(2,1)} %param.7, pred[4096]{0:T(1024)(128)(4,1)S(1)} %fusion.45), kind=kOutput, calls=%fused_computation.9 | convolution fusion | flops 2149580800 | bytes 5246976 | tf_op jit(solution)/shard_map/dot_general | solution.py:11
  9.6 2.6 %fusion.11 = f32[256,512]{1,0:T(8,128)} fusion(bf16[4096,256]{1,0:T(8,128)(2,1)S(1)} %copy-done, bf16[4096,512]{1,0:T(8,128)(2,1)S(1)} %copy-done.12, pred[4096]{0:T(1024)(128)(4,1)S(1)} %fusion.45), kind=kOutput, calls=%fused_computation.11 | convolution fusion | flops 1075838976 | bytes 6819840 | tf_op jit(solution)/shard_map/dot_general | solution.py:11
  12.2 2.3 %convolution_add_fusion = f32[512,512]{1,0:T(8,128)S(1)} fusion(f32[512,512]{1,0:T(8,128)} %fusion.8, f32[32,512]{1,0:T(8,128)S(1)} %copy-done.10, s32[]{:T(128)S(6)} %select_n.142), kind=kOutput, calls=%fused_computation.10 | convolution fusion | flops 50593792 | bytes 2129924 | tf_op jit(solution)/shard_map/dot_general | solution.py:11
  22.1 2.9 %collective-permute-start.1 = (f32[192,512]{1,0:T(8,128)S(1)}, f32[192,512]{1,0:T(8,128)S(1)}, u32[]{:S(2)}, u32[]{:S(2)}) collective-permute-start(f32[192,512]{1,0:T(8,128)S(1)} %slice_select_fusion.1), channel_id=1, source_target_pairs={{0,2},{1,3},{2,0},{3,1},{4,6},{5,7},{6,4},{7,5},{8,10},{9,11},{10,... | collective-permute-start | bytes 1179656 | tf_op jit(solution)/shard_map/ppermute | solution.py:31
  25.1 9.4 %collective-permute-done.1 = f32[192,512]{1,0:T(8,128)S(1)} collective-permute-done((f32[192,512]{1,0:T(8,128)S(1)}, f32[192,512]{1,0:T(8,128)S(1)}, u32[]{:S(2)}, u32[]{:S(2)}) %collective-permute-start.1) | collective-permute-done | bytes 393248 | tf_op jit(solution)/shard_map/ppermute | solution.py:31
  37.6 4.7 %collective-permute-done.2 = f32[96,512]{1,0:T(8,128)S(1)} collective-permute-done((f32[96,512]{1,0:T(8,128)S(1)}, f32[96,512]{1,0:T(8,128)S(1)}, u32[]{:S(2)}, u32[]{:S(2)}) %collective-permute-start.2) | collective-permute-done | bytes 196640 | tf_op jit(solution)/shard_map/ppermute | solution.py:31
  43.9 3.1 %collective-permute-done.3 = f32[48,512]{1,0:T(8,128)S(1)} collective-permute-done((f32[48,512]{1,0:T(8,128)S(1)}, f32[48,512]{1,0:T(8,128)S(1)}, u32[]{:S(2)}, u32[]{:S(2)}) %collective-permute-start.3) | collective-permute-done | bytes 98336 | tf_op jit(solution)/shard_map/ppermute | solution.py:31
  47.0 2.8 %collective-permute-start.4 = (f32[24,512]{1,0:T(8,128)S(1)}, f32[24,512]{1,0:T(8,128)S(1)}, u32[]{:S(2)}, u32[]{:S(2)}) collective-permute-start(f32[24,512]{1,0:T(8,128)S(1)} %slice_select_fusion.4), channel_id=1, source_target_pairs={{0,16},{1,17},{2,18},{3,19},{4,20},{5,21},{6,22},{7,23},{8,24},{9,... | collective-permute-start | bytes 147464 | tf_op jit(solution)/shard_map/ppermute | solution.py:31
  49.8 2.3 %collective-permute-done.4 = f32[24,512]{1,0:T(8,128)S(1)} collective-permute-done((f32[24,512]{1,0:T(8,128)S(1)}, f32[24,512]{1,0:T(8,128)S(1)}, u32[]{:S(2)}, u32[]{:S(2)}) %collective-permute-start.4) | collective-permute-done | bytes 49184 | tf_op jit(solution)/shard_map/ppermute | solution.py:31
  52.1 3.3 %collective-permute-start.5 = (f32[24,512]{1,0:T(8,128)S(1)}, f32[24,512]{1,0:T(8,128)S(1)}, u32[]{:S(2)}, u32[]{:S(2)}) collective-permute-start(f32[24,512]{1,0:T(8,128)S(1)} %select_add_fusion.4), channel_id=1, source_target_pairs={{0,16},{1,17},{2,18},{3,19},{4,20},{5,21},{6,22},{7,23},{8,24},{9,... | collective-permute-start | bytes 147464 | tf_op jit(solution)/shard_map/ppermute | solution.py:35
  57.5 2.8 %collective-permute-start.6 = (f32[48,512]{1,0:T(8,128)S(1)}, f32[48,512]{1,0:T(8,128)S(1)}, u32[]{:S(2)}, u32[]{:S(2)}) collective-permute-start(f32[48,512]{1,0:T(8,128)S(1)} %maximum_select_fusion.4), channel_id=1, source_target_pairs={{0,8},{1,9},{2,10},{3,11},{4,12},{5,13},{6,14},{7,15},{8,0},{9,1},... | collective-permute-start | bytes 294920 | tf_op jit(solution)/shard_map/ppermute | solution.py:35
  60.3 2.6 %collective-permute-done.6 = f32[48,512]{1,0:T(8,128)S(1)} collective-permute-done((f32[48,512]{1,0:T(8,128)S(1)}, f32[48,512]{1,0:T(8,128)S(1)}, u32[]{:S(2)}, u32[]{:S(2)}) %collective-permute-start.6) | collective-permute-done | bytes 98336 | tf_op jit(solution)/shard_map/ppermute | solution.py:35
  64.4 4.2 %collective-permute-done.7 = f32[96,512]{1,0:T(8,128)S(1)} collective-permute-done((f32[96,512]{1,0:T(8,128)S(1)}, f32[96,512]{1,0:T(8,128)S(1)}, u32[]{:S(2)}, u32[]{:S(2)}) %collective-permute-start.7) | collective-permute-done | bytes 196640 | tf_op jit(solution)/shard_map/ppermute | solution.py:35
  70.2 6.3 %collective-permute-done.8 = f32[192,512]{1,0:T(8,128)S(1)} collective-permute-done((f32[192,512]{1,0:T(8,128)S(1)}, f32[192,512]{1,0:T(8,128)S(1)}, u32[]{:S(2)}, u32[]{:S(2)}) %collective-permute-start.8) | collective-permute-done | bytes 393248 | tf_op jit(solution)/shard_map/ppermute | solution.py:35
  76.7 2.3 %collective-permute-done.9 = f32[384,512]{1,0:T(8,128)S(1)} collective-permute-done((f32[384,512]{1,0:T(8,128)S(1)}, f32[384,512]{1,0:T(8,128)S(1)}, u32[]{:S(2)}, u32[]{:S(2)}) %collective-permute-start.9) | collective-permute-done | bytes 786464 | tf_op jit(solution)/shard_map/ppermute | solution.py:35
  83.5 11.7 %custom-call.22 = f32[128,128]{1,0:T(8,128)S(1)} custom-call(f32[128,128]{1,0:T(8,128)S(1)} %copy.8), custom_call_target="Cholesky" | custom-call | tf_op jit(solution)/shard_map/cholesky/custom-call.1 | solution.py:71
  96.6 10.6 %custom-call.15 = f32[1,128,128]{1,2,0:T(8,128)} custom-call(f32[1,128,128]{2,1,0:T(8,128)S(1)} %get-tuple-element.11), custom_call_target="InvertDiagBlocksLowerTriangular" | custom-call | tf_op jit(solution)/shard_map/triangular_solve | solution.py:73
  110.5 11.7 %custom-call.23 = f32[128,128]{1,0:T(8,128)S(1)} custom-call(f32[128,128]{1,0:T(8,128)S(1)} %slice.151), custom_call_target="Cholesky" | custom-call | tf_op jit(solution)/shard_map/cholesky/custom-call.1 | solution.py:71
  123.5 9.8 %custom-call.16 = f32[1,128,128]{1,2,0:T(8,128)S(1)} custom-call(f32[1,128,128]{2,1,0:T(8,128)S(1)} %get-tuple-element.9), custom_call_target="InvertDiagBlocksLowerTriangular" | custom-call | tf_op jit(solution)/shard_map/triangular_solve | solution.py:73
  136.4 11.9 %custom-call.24 = f32[128,128]{1,0:T(8,128)S(1)} custom-call(f32[128,128]{1,0:T(8,128)S(1)} %slice.154), custom_call_target="Cholesky" | custom-call | tf_op jit(solution)/shard_map/cholesky/custom-call.1 | solution.py:71
  149.7 9.8 %custom-call.17 = f32[1,128,128]{1,2,0:T(8,128)S(1)} custom-call(f32[1,128,128]{2,1,0:T(8,128)S(1)} %get-tuple-element.7), custom_call_target="InvertDiagBlocksLowerTriangular" | custom-call | tf_op jit(solution)/shard_map/triangular_solve | solution.py:73
  162.7 11.7 %custom-call.25 = f32[128,128]{1,0:T(8,128)S(1)} custom-call(f32[128,128]{1,0:T(8,128)S(1)} %slice.157), custom_call_target="Cholesky" | custom-call | tf_op jit(solution)/shard_map/cholesky/custom-call.1 | solution.py:71
  177.5 2.6 %copy.11 = f32[512,512]{1,0:T(8,128)} copy(f32[512,512]{0,1:T(8,128)} %fusion.14) | data formatting | bytes 2097152
  180.1 10.6 %custom-call.18 = f32[1,128,128]{1,2,0:T(8,128)S(1)} custom-call(f32[1,128,128]{2,1,0:T(8,128)} %get-tuple-element.5), custom_call_target="InvertDiagBlocksLowerTriangular" | custom-call | tf_op jit(solution)/shard_map/triangular_solve | solution.py:73
  (87 shorter events, 41.0 us)
Async XLA Ops:
  0.6 8.9 %copy-start = (bf16[4096,256]{1,0:T(8,128)(2,1)S(1)}, bf16[4096,256]{1,0:T(8,128)(2,1)}, u32[]{:S(2)}) copy-start(bf16[4096,256]{1,0:T(8,128)(2,1)} %param.8) | copy-start | bytes 6291460
  2.2 7.4 %copy-start.12 = (bf16[4096,512]{1,0:T(8,128)(2,1)S(1)}, bf16[4096,512]{1,0:T(8,128)(2,1)}, u32[]{:S(2)}) copy-start(bf16[4096,512]{1,0:T(8,128)(2,1)} %param.7) | copy-start | bytes 12582916
  9.6 2.6 %copy-start.10 = (f32[32,512]{1,0:T(8,128)S(1)}, f32[32,512]{1,0:T(8,128)}, u32[]{:S(2)}) copy-start(f32[32,512]{1,0:T(8,128)} %param.11) | copy-start | bytes 196612
  12.1 2.3 %copy-start.11 = (f32[32,256]{1,0:T(8,128)S(1)}, f32[32,256]{1,0:T(8,128)}, u32[]{:S(2)}) copy-start(f32[32,256]{1,0:T(8,128)} %param.12) | copy-start | bytes 98308
  12.2 2.3 %copy-start.8 = (f32[256,512]{1,0:T(8,128)S(1)}, f32[256,512]{1,0:T(8,128)}, u32[]{:S(2)}) copy-start(f32[256,512]{1,0:T(8,128)} %fusion.11) | copy-start | bytes 1572868
  17.0 2.7 %collective-permute-start = (f32[384,512]{1,0:T(8,128)}, f32[384,512]{1,0:T(8,128)}, u32[]{:S(2)}, u32[]{:S(2)}) collective-permute-start(f32[384,512]{1,0:T(8,128)} %slice_select_fusion), channel_id=1, source_target_pairs={{0,1},{1,0},{2,3},{3,2},{4,5},{5,4},{6,7},{7,6},{8,9},{9,8},{10,11... | collective-permute-start | bytes 2359304 | tf_op jit(solution)/shard_map/ppermute | solution.py:31
  21.2 0.9 copy-start.1
  22.1 12.3 %collective-permute-start.1 = (f32[192,512]{1,0:T(8,128)S(1)}, f32[192,512]{1,0:T(8,128)S(1)}, u32[]{:S(2)}, u32[]{:S(2)}) collective-permute-start(f32[192,512]{1,0:T(8,128)S(1)} %slice_select_fusion.1), channel_id=1, source_target_pairs={{0,2},{1,3},{2,0},{3,1},{4,6},{5,7},{6,4},{7,5},{8,10},{9,11},{10,... | collective-permute-start | bytes 1179656 | tf_op jit(solution)/shard_map/ppermute | solution.py:31
  35.7 6.5 %collective-permute-start.2 = (f32[96,512]{1,0:T(8,128)S(1)}, f32[96,512]{1,0:T(8,128)S(1)}, u32[]{:S(2)}, u32[]{:S(2)}) collective-permute-start(f32[96,512]{1,0:T(8,128)S(1)} %slice_select_fusion.2), channel_id=1, source_target_pairs={{0,4},{1,5},{2,6},{3,7},{4,0},{5,1},{6,2},{7,3},{8,12},{9,13},{10,... | collective-permute-start | bytes 589832 | tf_op jit(solution)/shard_map/ppermute | solution.py:31
  42.3 4.7 %collective-permute-start.3 = (f32[48,512]{1,0:T(8,128)S(1)}, f32[48,512]{1,0:T(8,128)S(1)}, u32[]{:S(2)}, u32[]{:S(2)}) collective-permute-start(f32[48,512]{1,0:T(8,128)S(1)} %slice_select_fusion.3), channel_id=1, source_target_pairs={{0,8},{1,9},{2,10},{3,11},{4,12},{5,13},{6,14},{7,15},{8,0},{9,1},... | collective-permute-start | bytes 294920 | tf_op jit(solution)/shard_map/ppermute | solution.py:31
  47.0 5.1 %collective-permute-start.4 = (f32[24,512]{1,0:T(8,128)S(1)}, f32[24,512]{1,0:T(8,128)S(1)}, u32[]{:S(2)}, u32[]{:S(2)}) collective-permute-start(f32[24,512]{1,0:T(8,128)S(1)} %slice_select_fusion.4), channel_id=1, source_target_pairs={{0,16},{1,17},{2,18},{3,19},{4,20},{5,21},{6,22},{7,23},{8,24},{9,... | collective-permute-start | bytes 147464 | tf_op jit(solution)/shard_map/ppermute | solution.py:31
  52.1 5.4 %collective-permute-start.5 = (f32[24,512]{1,0:T(8,128)S(1)}, f32[24,512]{1,0:T(8,128)S(1)}, u32[]{:S(2)}, u32[]{:S(2)}) collective-permute-start(f32[24,512]{1,0:T(8,128)S(1)} %select_add_fusion.4), channel_id=1, source_target_pairs={{0,16},{1,17},{2,18},{3,19},{4,20},{5,21},{6,22},{7,23},{8,24},{9,... | collective-permute-start | bytes 147464 | tf_op jit(solution)/shard_map/ppermute | solution.py:35
  57.5 5.4 %collective-permute-start.6 = (f32[48,512]{1,0:T(8,128)S(1)}, f32[48,512]{1,0:T(8,128)S(1)}, u32[]{:S(2)}, u32[]{:S(2)}) collective-permute-start(f32[48,512]{1,0:T(8,128)S(1)} %maximum_select_fusion.4), channel_id=1, source_target_pairs={{0,8},{1,9},{2,10},{3,11},{4,12},{5,13},{6,14},{7,15},{8,0},{9,1},... | collective-permute-start | bytes 294920 | tf_op jit(solution)/shard_map/ppermute | solution.py:35
  62.9 5.7 %collective-permute-start.7 = (f32[96,512]{1,0:T(8,128)S(1)}, f32[96,512]{1,0:T(8,128)S(1)}, u32[]{:S(2)}, u32[]{:S(2)}) collective-permute-start(f32[96,512]{1,0:T(8,128)S(1)} %maximum_select_fusion.3), channel_id=1, source_target_pairs={{0,4},{1,5},{2,6},{3,7},{4,0},{5,1},{6,2},{7,3},{8,12},{9,13},{10,... | collective-permute-start | bytes 589832 | tf_op jit(solution)/shard_map/ppermute | solution.py:35
  68.7 7.8 %collective-permute-start.8 = (f32[192,512]{1,0:T(8,128)S(1)}, f32[192,512]{1,0:T(8,128)S(1)}, u32[]{:S(2)}, u32[]{:S(2)}) collective-permute-start(f32[192,512]{1,0:T(8,128)S(1)} %maximum_select_fusion.2), channel_id=1, source_target_pairs={{0,2},{1,3},{2,0},{3,1},{4,6},{5,7},{6,4},{7,5},{8,10},{9,11},{10,... | collective-permute-start | bytes 1179656 | tf_op jit(solution)/shard_map/ppermute | solution.py:35
  76.6 2.4 %collective-permute-start.9 = (f32[384,512]{1,0:T(8,128)S(1)}, f32[384,512]{1,0:T(8,128)S(1)}, u32[]{:S(2)}, u32[]{:S(2)}) collective-permute-start(f32[384,512]{1,0:T(8,128)S(1)} %maximum_select_fusion.1), channel_id=1, source_target_pairs={{0,1},{1,0},{2,3},{3,2},{4,5},{5,4},{6,7},{7,6},{8,9},{9,8},{10,11... | collective-permute-start | bytes 2359304 | tf_op jit(solution)/shard_map/ppermute | solution.py:35
  107.2 1.4 copy-start.4
  108.6 67.8 %copy-start.2 = (f32[640,128]{1,0:T(8,128)}, f32[640,128]{1,0:T(8,128)S(1)}, u32[]{:S(2)}) copy-start(f32[640,128]{1,0:T(8,128)S(1)} %fusion.18) | copy-start | bytes 983044
  109.5 0.9 copy-start.6
  134.7 41.7 %copy-start.5 = (f32[512,128]{1,0:T(8,128)}, f32[512,128]{1,0:T(8,128)S(1)}, u32[]{:S(2)}) copy-start(f32[512,128]{1,0:T(8,128)S(1)} %fusion.22) | copy-start | bytes 786436
  136.4 13.3 %copy-start.7 = (f32[512,256]{1,0:T(8,128)}, f32[512,256]{1,0:T(8,128)S(1)}, u32[]{:S(2)}) copy-start(f32[512,256]{1,0:T(8,128)S(1)} %convolution_subtract_fusion) | copy-start | bytes 1572868
  176.4 14.6 %slice-start.1 = ((f32[512,128]{1,0:T(8,128)}), f32[256,128]{1,0:T(8,128)S(1)}, s32[]{:S(2)}) async-start(f32[512,128]{1,0:T(8,128)} %copy-done.5), calls=%async_computation.1 | async-start | bytes 262144 | tf_op jit(solution)/shard_map/slice | solution.py:90
  177.5 13.5 %slice-start = ((f32[640,128]{1,0:T(8,128)}), f32[256,128]{1,0:T(8,128)S(1)}, s32[]{:S(2)}) async-start(f32[640,128]{1,0:T(8,128)} %copy-done.2), calls=%async_computation | async-start | bytes 262144 | tf_op jit(solution)/shard_map/slice | solution.py:90
  177.5 13.5 %copy-start.9 = (f32[256,128]{1,0:T(8,128)S(1)}, f32[256,128]{1,0:T(8,128)}, u32[]{:S(2)}) copy-start(f32[256,128]{1,0:T(8,128)} %slice.160) | copy-start | bytes 393220
  (1 other events, 0.8 us)
